TPU v7x, 512 devices: a whole 4x4x16 slice. The times are simulated.
512 devices in a mesh: row: 32 (over x, y, core), col: 16 (over z).
Axes of the slice: x: 4, y: 4, z: 16, core: 2. Of those that a mesh axis runs over, the one named last changes fastest.
Arguments:
- panel: float32 [65536, 256], P('row', 'col'), may hold values from -210 to 210
- slab: float32 [65536, 4096], P('row', 'col'), may hold values from -6 to 6
Outputs:
- triangle: float32 [256, 256], P(None, 'col')
- projected: float32 [256, 4096], P(None, 'col')
- residual: float32 [65536, 4096], P('row', 'col')
All inputs are finite; a program needn't handle non-finite values.
Results may differ from a plain program's by a relative error of at most 0.0003.
Values sent between devices are 32-bit elements; how exact they have to be, the bound alone decides.
No kernel may reach another device: no remote copies, remote signals or barrier semaphores. Data moves between devices by JAX's collectives and lax.ppermute only.
A program may use at most 64 MiB of HBM per device.

v0:
```python
import math
import jax
import jax.numpy as jnp
from jax import lax
from jax.sharding import PartitionSpec as P

contract_rows = (((0,), (0,)), ((), ()))


def per_device(panel, slab):
    highest = lax.Precision.HIGHEST
    gathered = lax.all_gather(panel, "col", axis=1, tiled=True)
    cross_local = lax.dot_general(gathered, slab, contract_rows, precision=highest)
    gram_local = lax.dot_general(gathered, gathered, contract_rows, precision=highest)
    gram_total, totals = lax.psum((gram_local, cross_local), "row")
    lower_factor = jnp.linalg.cholesky(gram_total)
    projected = lax.linalg.triangular_solve(
        lower_factor, totals, left_side=True, lower=True, transpose_a=False
    )
    basis_rows = lax.linalg.triangular_solve(
        lower_factor, gathered, left_side=False, lower=True, transpose_a=True
    )
    residual = slab - jnp.dot(basis_rows, projected, precision=highest)
    col_width = panel.shape[1]
    rows_total = gathered.shape[0] * lax.axis_size("row")
    scaled = lower_factor.T * (1.0 / math.sqrt(rows_total))
    triangle = lax.dynamic_slice_in_dim(scaled, lax.axis_index("col") * col_width, col_width, 1)
    return (triangle, projected, residual)


def solution(mesh):
    placed = (P("row", "col"), P("row", "col"))
    return jax.shard_map(
        per_device,
        mesh=mesh,
        in_specs=placed,
        out_specs=(P(None, "col"), P(None, "col"), P("row", "col")),
        check_vma=False,
    )
```

profile of v0, /device:TPU:1, one launch (start us, length us, event | category | flops | bytes accessed | tf_op | source)
XLA Modules:
  0.0 307.3 jit_solution(13206898415730622074)
XLA Ops:
  7.2 0.0 all-gather.2.cloned.1.call-start
  7.2 0.7 all-gather.2.cloned.1.call-update
  7.9 0.0 all-reduce.4.cloned.1.call-start
  7.9 71.5 %all-gather.2.cloned.1.call-done = f32[2048,256]{0,1:T(8,128)} async-done(((f32[2048,16]{0,1:T(8,128)}), f32[2048,256]{0,1:T(8,128)}) %all-gather.2.cloned.1.call-update) | async-done | bytes 2097168 | tf_op jit(solution)/shard_map/all_gather | solution.py:12
  79.5 0.0 copy-start
  79.5 4.9 %fusion.19 = f32[256,256]{0,1:T(8,128)} fusion(f32[2048,256]{0,1:T(8,128)} %all-gather.2.cloned.1.call-done), kind=kOutput, calls=%fused_computation.42 | convolution fusion | flops 1610612736 | bytes 2359296 | tf_op jit(solution)/shard_map/dot_general | solution.py:14
  84.4 0.0 copy-done
  84.4 4.2 %fusion.20 = f32[256,256]{1,0:T(8,128)} fusion(f32[2048,256]{0,1:T(8,128)S(1)} %copy-done, f32[2048,256]{1,0:T(8,128)} %param.3), kind=kOutput, calls=%fused_computation.43 | convolution fusion | flops 1610612736 | bytes 4456448 | tf_op jit(solution)/shard_map/dot_general | solution.py:13
  88.6 0.0 all-reduce.4.cloned.1.call-update
  88.6 140.3 %all-reduce.4.cloned.1.call-done = (f32[256,256]{0,1:T(8,128)}, f32[256,256]{1,0:T(8,128)}) async-done(((f32[256,256]{0,1:T(8,128)}, f32[256,256]{1,0:T(8,128)}), (f32[256,256]{0,1:T(8,128)}, f32[256,256]{1,0:T(8,128)})) %all-reduce.4.cloned.1.call-update) | async-done | bytes 524304 | tf_op jit(solution)/shard_map/psum | solution.py:15
  228.9 0.0 copy-start.3
  228.9 1.1 copy.6
  230.1 1.0 fusion.5
  231.1 11.7 %cholesky.50 = f32[128,128]{1,0:T(8,128)S(1)} custom-call(f32[128,128]{1,0:T(8,128)S(1)} %cholesky.118), custom_call_target="Cholesky" | custom-call | tf_op jit(solution)/shard_map/jit(cholesky)/cholesky | solution.py:16
  242.8 9.8 %custom-call.16 = f32[1,128,128]{1,2,0:T(8,128)S(1)} custom-call(f32[1,128,128]{2,1,0:T(8,128)S(1)} %get-tuple-element.28), custom_call_target="InvertDiagBlocksLowerTriangular" | custom-call | tf_op jit(solution)/shard_map/jit(cholesky)/cholesky | solution.py:16
  252.7 0.2 constant_dynamic-update-slice_fusion
  252.9 0.3 convolution_subtract_fusion.3
  253.2 11.9 %cholesky.105 = f32[128,128]{1,0:T(8,128)S(1)} custom-call(f32[128,128]{1,0:T(8,128)S(1)} %convolution_subtract_fusion.3), custom_call_target="Cholesky" | custom-call | tf_op jit(solution)/shard_map/jit(cholesky)/cholesky | solution.py:16
  265.1 0.6 compare_reduce_fusion
  267.1 0.1 triangular_solve.59
  267.1 4.0 %while.1 = (s32[]{:T(128)}, f32[256,256]{1,0:T(8,128)S(1)}, s32[2,2]{1,0:T(2,128)S(1)}, f32[2,128,128]{2,1,0:T(8,128)S(1)}, s32[]{:T(128)}) while((s32[]{:T(128)}, f32[256,256]{1,0:T(8,128)S(1)}, s32[2,2]{1,0:T(2,128)S(1)}, f32[2,128,128]{2,1,0:T(8,128)S(1)}, s32[]{:T(128)}) %tuple.28), condition=%wide.while_cond, body=%wide.while_body.sunk | while | flops 2 | bytes 131189 | solution.py:17
  267.1 0.6 fusion.33
  267.7 1.4 bitcast_dynamic-update-slice_fusion.2
  269.1 0.6 fusion.33
  269.7 1.4 bitcast_dynamic-update-slice_fusion.2
  271.1 19.7 %custom-call.17 = f32[2,128,128]{1,2,0:T(8,128)S(1)} custom-call(f32[2,128,128]{2,1,0:T(8,128)S(1)} %get-tuple-element.10), custom_call_target="InvertDiagBlocksLowerTriangular" | custom-call | tf_op jit(solution)/shard_map/triangular_solve | solution.py:17
  290.8 0.0 copy-done.3
  290.8 0.3 fusion.7
  291.1 0.3 convolution_subtract_fusion.2
  291.4 0.3 fusion.13
  291.8 0.0 copy-start.2
  291.8 1.0 fusion.3
  292.8 0.0 copy-start.1
  292.8 1.1 convolution_subtract_fusion.1
  293.9 1.1 fusion.12
  295.0 0.6 fusion.16
  295.6 0.0 copy-done.2
  295.6 0.0 copy-done.1
  295.6 4.9 %convolution_subtract_fusion = f32[2048,256]{1,0:T(8,128)} fusion(f32[2048,256]{1,0:T(8,128)S(1)} %copy-done.1, f32[256,256]{1,0:T(8,128)S(1)} %pad_maximum_fusion, f32[2048,128]{0,1:T(8,128)S(1)} %fusion.12, f32[2048,128]{0,1:T(8,128)S(1)} %bitcast.43), kind=kOutput, calls=%fused_computation.2 | convolution fusion | flops 1611661312 | bytes 6553600 | tf_op jit(solution)/shard_map/dot_general | solution.py:23
  (10 shorter events, 0.2 us)
Async XLA Ops:
  7.2 72.3 %all-gather.2.cloned.1.call-start = ((), (), s32[]{:S(2)}) async-start(), calls=%async_computation | async-start | bytes 2228224 | tf_op jit(solution)/shard_map/all_gather | solution.py:12
  7.9 221.0 %all-reduce.4.cloned.1.call-start = ((), (), s32[]{:S(2)}) async-start(), calls=%async_computation.1 | async-start | bytes 1048576 | tf_op jit(solution)/shard_map/psum | solution.py:15
  79.5 4.9 %copy-start = (f32[2048,256]{0,1:T(8,128)S(1)}, f32[2048,256]{0,1:T(8,128)}, u32[]{:S(2)}) copy-start(f32[2048,256]{0,1:T(8,128)} %all-gather.2.cloned.1.call-done) | copy-start | bytes 6291460
  228.9 61.9 %copy-start.3 = (f32[256,256]{1,0:T(8,128)S(1)}, f32[256,256]{1,0:T(8,128)}, u32[]{:S(2)}) copy-start(f32[256,256]{1,0:T(8,128)} %get-tuple-element.20) | copy-start | bytes 786436
  291.8 3.9 %copy-start.2 = (f32[256,256]{1,0:T(8,128)}, f32[256,256]{1,0:T(8,128)S(1)}, u32[]{:S(2)}) copy-start(f32[256,256]{1,0:T(8,128)S(1)} %pad_maximum_fusion) | copy-start | bytes 786436
  292.8 2.8 copy-start.1
Sparse Core Ops, SparseCore 0:
  10.1 69.3 all-gather.1
  88.7 140.1 all-reduce.3
where the time goes:
time: 308 us; the launch traced here: 307 us
  waiting for transfers between devices  213 us (69%)
  other arithmetic  55.5 us (18%)
  matrix products  18.5 us (6%)
  between operations  15.5 us (5%)
  local copies, waits for them, and re-layouts  5.19 us (2%)
    psum x1, waiting for transfers between devices, per_device(): gram_total, totals = lax.psum((gram_local, cross_local), 'row')  140 us
    all_gather x1, waiting for transfers between devices, per_device(): gathered = lax.all_gather(panel, 'col', axis=1, tiled=True)  71.5 us
    another operation x6, other arithmetic, per_device(): lower_factor = jnp.linalg.cholesky(gram_total)  34.1 us
    another operation x4, other arithmetic, per_device(): lax.linalg.triangular_solve(lower_factor, totals, left_side=True, lower=T...  19.7 us
  transfers between devices with their start and end apart: 2, of which 2 were waited for; matrix products, arithmetic and copies ran while one was open for 0% of the time, Pallas kernels for 0%

commit v1 on v0

--- a/solution.py
+++ b/solution.py
@@ -9,7 +9,19 @@
 
 def per_device(panel, slab):
     highest = lax.Precision.HIGHEST
-    gathered = lax.all_gather(panel, "col", axis=1, tiled=True)
+    ways, here, lap = (lax.axis_size("col"), lax.axis_index("col"), panel.shape[1])
+    shape = [n * ways if d == 1 else n for d, n in enumerate(panel.shape)]
+    full = lax.dynamic_update_slice_in_dim(jnp.zeros(shape, panel.dtype), panel, here * lap, axis=1)
+    going_up = going_down = panel
+    for far in range(1, ways // 2 + 1):
+        going_up = lax.ppermute(going_up, "col", [(d, (d + 1) % ways) for d in range(ways)])
+        full = lax.dynamic_update_slice_in_dim(full, going_up, (here - far) % ways * lap, axis=1)
+        if 2 * far < ways:
+            going_down = lax.ppermute(going_down, "col", [(d, (d - 1) % ways) for d in range(ways)])
+            full = lax.dynamic_update_slice_in_dim(
+                full, going_down, (here + far) % ways * lap, axis=1
+            )
+    gathered = full
     cross_local = lax.dot_general(gathered, slab, contract_rows, precision=highest)
     gram_local = lax.dot_general(gathered, gathered, contract_rows, precision=highest)
     gram_total, totals = lax.psum((gram_local, cross_local), "row")

time: 308 us -> 298 us (0.968)
  waiting for transfers between devices: 213 us -> 151 us
  starting transfers between devices: 0.08 us -> 54.7 us
  matrix products: 18.5 us -> 14.7 us
    all_gather x1 -> x0, waiting for transfers between devices: 71.5 us -> none  [per_device(): gathered = lax.all_gather(panel, 'col', axis=1, tiled=True)]
    ppermute x0 -> x15, starting transfers between devices: none -> 54.7 us  [the longest x7 36.9 us: per_device(): lax.ppermute(going_down, 'col', [(d, (d - 1) % ways) for d in range(ways)])]
    ppermute x0 -> x15, waiting for transfers between devices: none -> 9.91 us  [the longest x8 9.9 us: per_device(): lax.ppermute(going_up, 'col', [(d, (d + 1) % ways) for d in range(ways)])]
  transfers between devices with their start and end apart: 2 -> 16, of which waited for: 2 -> 9; matrix products, arithmetic and copies ran while one was open for 0% -> 0% of each run, Pallas kernels for 0% -> 0%
where the time goes in v1:
time: 298 us
  waiting for transfers between devices  151 us (51%)
  other arithmetic  55.5 us (19%)
  starting transfers between devices  54.7 us (18%)
  between operations  16.1 us (5%)
  matrix products  14.7 us (5%)
  local copies, waits for them, and re-layouts  6.08 us (2%)
    psum x1, waiting for transfers between devices, per_device(): gram_total, totals = lax.psum((gram_local, cross_local), 'row')  141 us
    ppermute x7, starting transfers between devices, per_device(): lax.ppermute(going_down, 'col', [(d, (d - 1) % ways) for d in range(ways)])  36.9 us
    another operation x6, other arithmetic, per_device(): lower_factor = jnp.linalg.cholesky(gram_total)  34.1 us
    another operation x4, other arithmetic, per_device(): lax.linalg.triangular_solve(lower_factor, totals, left_side=True, lower=T...  19.7 us
    ppermute x8, starting transfers between devices, per_device(): lax.ppermute(going_up, 'col', [(d, (d + 1) % ways) for d in range(ways)])  17.7 us
    ppermute x8, waiting for transfers between devices, per_device(): lax.ppermute(going_up, 'col', [(d, (d + 1) % ways) for d in range(ways)])  9.9 us
  transfers between devices with their start and end apart: 16, of which 9 were waited for; matrix products, arithmetic and copies ran while one was open for 0% of the time, Pallas kernels for 0%

profile of v1, /device:TPU:1, one launch (start us, length us, event | category | flops | bytes accessed | tf_op | source)
XLA Modules:
  0.0 297.7 jit_solution(11310904592474972377)
XLA Ops:
  7.2 4.4 %collective-permute-start = (f32[2048,16]{0,1:T(8,128)}, f32[2048,16]{0,1:T(8,128)S(1)}, u32[]{:S(2)}, u32[]{:S(2)}) collective-permute-start(f32[2048,16]{0,1:T(8,128)} %param.2), channel_id=1, source_target_pairs={{0,1},{1,2},{2,3},{3,4},{4,5},{5,6},{6,7},{7,8},{8,9},{9,10},{10,1... | collective-permute-start | bytes 393224 | tf_op jit(solution)/shard_map/ppermute | solution.py:17
  11.6 9.5 %collective-permute-start.1 = (f32[2048,16]{0,1:T(8,128)}, f32[2048,16]{0,1:T(8,128)S(1)}, u32[]{:S(2)}, u32[]{:S(2)}) collective-permute-start(f32[2048,16]{0,1:T(8,128)} %param.2), channel_id=1, source_target_pairs={{0,15},{1,0},{2,1},{3,2},{4,3},{5,4},{6,5},{7,6},{8,7},{9,8},{10,9... | collective-permute-start | bytes 393224 | tf_op jit(solution)/shard_map/ppermute | solution.py:20
  21.7 0.9 collective-permute-done
  22.6 1.9 collective-permute-start.2
  24.5 4.6 %collective-permute-start.3 = (f32[2048,16]{0,1:T(8,128)S(1)}, f32[2048,16]{0,1:T(8,128)S(1)}, u32[]{:S(2)}, u32[]{:S(2)}) collective-permute-start(f32[2048,16]{0,1:T(8,128)S(1)} %collective-permute-done.1), channel_id=1, source_target_pairs={{0,15},{1,0},{2,1},{3,2},{4,3},{5,4},{6,5},{7,6},{8,7},{9,8},{10,9... | collective-permute-start | bytes 393224 | tf_op jit(solution)/shard_map/ppermute | solution.py:20
  29.2 0.4 collective-permute-done.2
  29.5 1.9 collective-permute-start.4
  31.4 4.6 %collective-permute-start.5 = (f32[2048,16]{0,1:T(8,128)S(1)}, f32[2048,16]{0,1:T(8,128)S(1)}, u32[]{:S(2)}, u32[]{:S(2)}) collective-permute-start(f32[2048,16]{0,1:T(8,128)S(1)} %collective-permute-done.3), channel_id=1, source_target_pairs={{0,15},{1,0},{2,1},{3,2},{4,3},{5,4},{6,5},{7,6},{8,7},{9,8},{10,9... | collective-permute-start | bytes 393224 | tf_op jit(solution)/shard_map/ppermute | solution.py:20
  36.1 0.4 collective-permute-done.4
  36.4 1.9 collective-permute-start.6
  38.3 4.6 %collective-permute-start.7 = (f32[2048,16]{0,1:T(8,128)S(1)}, f32[2048,16]{0,1:T(8,128)S(1)}, u32[]{:S(2)}, u32[]{:S(2)}) collective-permute-start(f32[2048,16]{0,1:T(8,128)S(1)} %collective-permute-done.5), channel_id=1, source_target_pairs={{0,15},{1,0},{2,1},{3,2},{4,3},{5,4},{6,5},{7,6},{8,7},{9,8},{10,9... | collective-permute-start | bytes 393224 | tf_op jit(solution)/shard_map/ppermute | solution.py:20
  43.0 0.4 collective-permute-done.6
  43.3 1.9 collective-permute-start.8
  45.3 4.6 %collective-permute-start.9 = (f32[2048,16]{0,1:T(8,128)S(1)}, f32[2048,16]{0,1:T(8,128)S(1)}, u32[]{:S(2)}, u32[]{:S(2)}) collective-permute-start(f32[2048,16]{0,1:T(8,128)S(1)} %collective-permute-done.7), channel_id=1, source_target_pairs={{0,15},{1,0},{2,1},{3,2},{4,3},{5,4},{6,5},{7,6},{8,7},{9,8},{10,9... | collective-permute-start | bytes 393224 | tf_op jit(solution)/shard_map/ppermute | solution.py:20
  49.9 0.4 collective-permute-done.8
  50.2 1.9 collective-permute-start.10
  52.2 4.6 %collective-permute-start.11 = (f32[2048,16]{0,1:T(8,128)S(1)}, f32[2048,16]{0,1:T(8,128)S(1)}, u32[]{:S(2)}, u32[]{:S(2)}) collective-permute-start(f32[2048,16]{0,1:T(8,128)S(1)} %collective-permute-done.9), channel_id=1, source_target_pairs={{0,15},{1,0},{2,1},{3,2},{4,3},{5,4},{6,5},{7,6},{8,7},{9,8},{10,9... | collective-permute-start | bytes 393224 | tf_op jit(solution)/shard_map/ppermute | solution.py:20
  56.8 0.4 collective-permute-done.10
  57.2 1.9 collective-permute-start.12
  59.1 4.6 %collective-permute-start.13 = (f32[2048,16]{0,1:T(8,128)S(1)}, f32[2048,16]{0,1:T(8,128)S(1)}, u32[]{:S(2)}, u32[]{:S(2)}) collective-permute-start(f32[2048,16]{0,1:T(8,128)S(1)} %collective-permute-done.11), channel_id=1, source_target_pairs={{0,15},{1,0},{2,1},{3,2},{4,3},{5,4},{6,5},{7,6},{8,7},{9,8},{10,9... | collective-permute-start | bytes 393224 | tf_op jit(solution)/shard_map/ppermute | solution.py:20
  63.7 1.1 collective-permute-done.12
  64.8 1.9 collective-permute-start.14
  66.8 6.1 %collective-permute-done.14 = f32[2048,16]{0,1:T(8,128)S(1)} collective-permute-done((f32[2048,16]{0,1:T(8,128)S(1)}, f32[2048,16]{0,1:T(8,128)S(1)}, u32[]{:S(2)}, u32[]{:S(2)}) %collective-permute-start.14) | collective-permute-done | bytes 131104 | tf_op jit(solution)/shard_map/ppermute | solution.py:17
  72.9 2.6 fusion.21
  75.5 2.6 fusion.22
  78.1 140.6 %all-reduce.4.cloned.1.call-done = (f32[256,256]{0,1:T(8,128)}, f32[256,256]{1,0:T(8,128)}) async-done(((f32[256,256]{0,1:T(8,128)}, f32[256,256]{1,0:T(8,128)}), (f32[256,256]{0,1:T(8,128)}, f32[256,256]{1,0:T(8,128)})) %all-reduce.4.cloned.1.call-update) | async-done | bytes 524304 | tf_op jit(solution)/shard_map/psum | solution.py:27
  218.8 1.1 copy.6
  219.9 1.0 fusion.6
  220.9 11.7 %cholesky.50 = f32[128,128]{1,0:T(8,128)S(1)} custom-call(f32[128,128]{1,0:T(8,128)S(1)} %cholesky.118), custom_call_target="Cholesky" | custom-call | tf_op jit(solution)/shard_map/jit(cholesky)/cholesky | solution.py:28
  232.7 9.8 %custom-call.16 = f32[1,128,128]{1,2,0:T(8,128)S(1)} custom-call(f32[1,128,128]{2,1,0:T(8,128)S(1)} %get-tuple-element.28), custom_call_target="InvertDiagBlocksLowerTriangular" | custom-call | tf_op jit(solution)/shard_map/jit(cholesky)/cholesky | solution.py:28
  242.7 0.3 convolution_subtract_fusion.1
  243.0 11.9 %cholesky.105 = f32[128,128]{1,0:T(8,128)S(1)} custom-call(f32[128,128]{1,0:T(8,128)S(1)} %convolution_subtract_fusion.1), custom_call_target="Cholesky" | custom-call | tf_op jit(solution)/shard_map/jit(cholesky)/cholesky | solution.py:28
  254.9 0.6 compare_reduce_fusion
  256.9 0.6 fusion.18
  257.6 4.0 %while.1 = (s32[]{:T(128)}, f32[256,256]{1,0:T(8,128)S(1)}, s32[2,2]{1,0:T(2,128)S(1)}, f32[2,128,128]{2,1,0:T(8,128)S(1)}, s32[]{:T(128)}) while((s32[]{:T(128)}, f32[256,256]{1,0:T(8,128)S(1)}, s32[2,2]{1,0:T(2,128)S(1)}, f32[2,128,128]{2,1,0:T(8,128)S(1)}, s32[]{:T(128)}) %tuple.28), condition=%wide.while_cond, body=%wide.while_body.sunk | while | flops 2 | bytes 131189 | solution.py:29
  257.6 0.6 fusion.33
  258.1 1.4 bitcast_dynamic-update-slice_fusion.2
  259.6 0.6 fusion.33
  260.1 1.4 bitcast_dynamic-update-slice_fusion.2
  261.5 19.7 %custom-call.17 = f32[2,128,128]{1,2,0:T(8,128)S(1)} custom-call(f32[2,128,128]{2,1,0:T(8,128)S(1)} %get-tuple-element.10), custom_call_target="InvertDiagBlocksLowerTriangular" | custom-call | tf_op jit(solution)/shard_map/triangular_solve | solution.py:29
  281.2 1.1 fusion.4
  282.3 0.3 fusion.9
  282.6 0.3 fusion.16
  282.9 0.3 fusion.8
  283.3 1.1 fusion.14
  284.4 1.1 fusion.3
  285.5 0.4 copy-done.1
  285.9 4.9 %convolution_subtract_fusion = f32[2048,256]{1,0:T(8,128)} fusion(f32[2048,256]{1,0:T(8,128)S(1)} %copy-done.1, f32[256,256]{1,0:T(8,128)S(1)} %pad_maximum_fusion, f32[2048,128]{0,1:T(8,128)S(1)} %fusion.3, f32[2048,128]{0,1:T(8,128)S(1)} %fusion.4), kind=kOutput, calls=%fused_computation.2 | convolution fusion | flops 1611661312 | bytes 6553600 | tf_op jit(solution)/shard_map/dot_general | solution.py:35
  (47 shorter events, 1.0 us)
Async XLA Ops:
  7.2 14.5 %copy-start.4 = (f32[2048,16]{0,1:T(8,128)S(1)}, f32[2048,16]{0,1:T(8,128)}, u32[]{:S(2)}) copy-start(f32[2048,16]{0,1:T(8,128)} %param.2) | copy-start | bytes 393220
  7.2 211.6 %all-reduce.4.cloned.1.call-start = ((), (), s32[]{:S(2)}) async-start(), calls=%async_computation | async-start | bytes 1048576 | tf_op jit(solution)/shard_map/psum | solution.py:27
  7.2 15.4 %collective-permute-start = (f32[2048,16]{0,1:T(8,128)}, f32[2048,16]{0,1:T(8,128)S(1)}, u32[]{:S(2)}, u32[]{:S(2)}) collective-permute-start(f32[2048,16]{0,1:T(8,128)} %param.2), channel_id=1, source_target_pairs={{0,1},{1,2},{2,3},{3,4},{4,5},{5,6},{6,7},{7,8},{8,9},{9,10},{10,1... | collective-permute-start | bytes 393224 | tf_op jit(solution)/shard_map/ppermute | solution.py:17
  11.6 12.9 %collective-permute-start.1 = (f32[2048,16]{0,1:T(8,128)}, f32[2048,16]{0,1:T(8,128)S(1)}, u32[]{:S(2)}, u32[]{:S(2)}) collective-permute-start(f32[2048,16]{0,1:T(8,128)} %param.2), channel_id=1, source_target_pairs={{0,15},{1,0},{2,1},{3,2},{4,3},{5,4},{6,5},{7,6},{8,7},{9,8},{10,9... | collective-permute-start | bytes 393224 | tf_op jit(solution)/shard_map/ppermute | solution.py:20
  22.6 6.9 %collective-permute-start.2 = (f32[2048,16]{0,1:T(8,128)S(1)}, f32[2048,16]{0,1:T(8,128)S(1)}, u32[]{:S(2)}, u32[]{:S(2)}) collective-permute-start(f32[2048,16]{0,1:T(8,128)S(1)} %collective-permute-done), channel_id=1, source_target_pairs={{0,1},{1,2},{2,3},{3,4},{4,5},{5,6},{6,7},{7,8},{8,9},{9,10},{10,1... | collective-permute-start | bytes 393224 | tf_op jit(solution)/shard_map/ppermute | solution.py:17
  24.5 6.9 %collective-permute-start.3 = (f32[2048,16]{0,1:T(8,128)S(1)}, f32[2048,16]{0,1:T(8,128)S(1)}, u32[]{:S(2)}, u32[]{:S(2)}) collective-permute-start(f32[2048,16]{0,1:T(8,128)S(1)} %collective-permute-done.1), channel_id=1, source_target_pairs={{0,15},{1,0},{2,1},{3,2},{4,3},{5,4},{6,5},{7,6},{8,7},{9,8},{10,9... | collective-permute-start | bytes 393224 | tf_op jit(solution)/shard_map/ppermute | solution.py:20
  29.5 6.9 %collective-permute-start.4 = (f32[2048,16]{0,1:T(8,128)S(1)}, f32[2048,16]{0,1:T(8,128)S(1)}, u32[]{:S(2)}, u32[]{:S(2)}) collective-permute-start(f32[2048,16]{0,1:T(8,128)S(1)} %collective-permute-done.2), channel_id=1, source_target_pairs={{0,1},{1,2},{2,3},{3,4},{4,5},{5,6},{6,7},{7,8},{8,9},{9,10},{10,1... | collective-permute-start | bytes 393224 | tf_op jit(solution)/shard_map/ppermute | solution.py:17
  31.4 6.9 %collective-permute-start.5 = (f32[2048,16]{0,1:T(8,128)S(1)}, f32[2048,16]{0,1:T(8,128)S(1)}, u32[]{:S(2)}, u32[]{:S(2)}) collective-permute-start(f32[2048,16]{0,1:T(8,128)S(1)} %collective-permute-done.3), channel_id=1, source_target_pairs={{0,15},{1,0},{2,1},{3,2},{4,3},{5,4},{6,5},{7,6},{8,7},{9,8},{10,9... | collective-permute-start | bytes 393224 | tf_op jit(solution)/shard_map/ppermute | solution.py:20
  36.4 6.9 %collective-permute-start.6 = (f32[2048,16]{0,1:T(8,128)S(1)}, f32[2048,16]{0,1:T(8,128)S(1)}, u32[]{:S(2)}, u32[]{:S(2)}) collective-permute-start(f32[2048,16]{0,1:T(8,128)S(1)} %collective-permute-done.4), channel_id=1, source_target_pairs={{0,1},{1,2},{2,3},{3,4},{4,5},{5,6},{6,7},{7,8},{8,9},{9,10},{10,1... | collective-permute-start | bytes 393224 | tf_op jit(solution)/shard_map/ppermute | solution.py:17
  38.3 6.9 %collective-permute-start.7 = (f32[2048,16]{0,1:T(8,128)S(1)}, f32[2048,16]{0,1:T(8,128)S(1)}, u32[]{:S(2)}, u32[]{:S(2)}) collective-permute-start(f32[2048,16]{0,1:T(8,128)S(1)} %collective-permute-done.5), channel_id=1, source_target_pairs={{0,15},{1,0},{2,1},{3,2},{4,3},{5,4},{6,5},{7,6},{8,7},{9,8},{10,9... | collective-permute-start | bytes 393224 | tf_op jit(solution)/shard_map/ppermute | solution.py:20
  43.3 6.9 %collective-permute-start.8 = (f32[2048,16]{0,1:T(8,128)S(1)}, f32[2048,16]{0,1:T(8,128)S(1)}, u32[]{:S(2)}, u32[]{:S(2)}) collective-permute-start(f32[2048,16]{0,1:T(8,128)S(1)} %collective-permute-done.6), channel_id=1, source_target_pairs={{0,1},{1,2},{2,3},{3,4},{4,5},{5,6},{6,7},{7,8},{8,9},{9,10},{10,1... | collective-permute-start | bytes 393224 | tf_op jit(solution)/shard_map/ppermute | solution.py:17
  45.3 6.9 %collective-permute-start.9 = (f32[2048,16]{0,1:T(8,128)S(1)}, f32[2048,16]{0,1:T(8,128)S(1)}, u32[]{:S(2)}, u32[]{:S(2)}) collective-permute-start(f32[2048,16]{0,1:T(8,128)S(1)} %collective-permute-done.7), channel_id=1, source_target_pairs={{0,15},{1,0},{2,1},{3,2},{4,3},{5,4},{6,5},{7,6},{8,7},{9,8},{10,9... | collective-permute-start | bytes 393224 | tf_op jit(solution)/shard_map/ppermute | solution.py:20
  50.2 6.9 %collective-permute-start.10 = (f32[2048,16]{0,1:T(8,128)S(1)}, f32[2048,16]{0,1:T(8,128)S(1)}, u32[]{:S(2)}, u32[]{:S(2)}) collective-permute-start(f32[2048,16]{0,1:T(8,128)S(1)} %collective-permute-done.8), channel_id=1, source_target_pairs={{0,1},{1,2},{2,3},{3,4},{4,5},{5,6},{6,7},{7,8},{8,9},{9,10},{10,1... | collective-permute-start | bytes 393224 | tf_op jit(solution)/shard_map/ppermute | solution.py:17
  52.2 6.9 %collective-permute-start.11 = (f32[2048,16]{0,1:T(8,128)S(1)}, f32[2048,16]{0,1:T(8,128)S(1)}, u32[]{:S(2)}, u32[]{:S(2)}) collective-permute-start(f32[2048,16]{0,1:T(8,128)S(1)} %collective-permute-done.9), channel_id=1, source_target_pairs={{0,15},{1,0},{2,1},{3,2},{4,3},{5,4},{6,5},{7,6},{8,7},{9,8},{10,9... | collective-permute-start | bytes 393224 | tf_op jit(solution)/shard_map/ppermute | solution.py:20
  57.2 7.7 %collective-permute-start.12 = (f32[2048,16]{0,1:T(8,128)S(1)}, f32[2048,16]{0,1:T(8,128)S(1)}, u32[]{:S(2)}, u32[]{:S(2)}) collective-permute-start(f32[2048,16]{0,1:T(8,128)S(1)} %collective-permute-done.10), channel_id=1, source_target_pairs={{0,1},{1,2},{2,3},{3,4},{4,5},{5,6},{6,7},{7,8},{8,9},{9,10},{10,1... | collective-permute-start | bytes 393224 | tf_op jit(solution)/shard_map/ppermute | solution.py:17
  59.1 7.7 %collective-permute-start.13 = (f32[2048,16]{0,1:T(8,128)S(1)}, f32[2048,16]{0,1:T(8,128)S(1)}, u32[]{:S(2)}, u32[]{:S(2)}) collective-permute-start(f32[2048,16]{0,1:T(8,128)S(1)} %collective-permute-done.11), channel_id=1, source_target_pairs={{0,15},{1,0},{2,1},{3,2},{4,3},{5,4},{6,5},{7,6},{8,7},{9,8},{10,9... | collective-permute-start | bytes 393224 | tf_op jit(solution)/shard_map/ppermute | solution.py:20
  64.8 8.1 %collective-permute-start.14 = (f32[2048,16]{0,1:T(8,128)S(1)}, f32[2048,16]{0,1:T(8,128)S(1)}, u32[]{:S(2)}, u32[]{:S(2)}) collective-permute-start(f32[2048,16]{0,1:T(8,128)S(1)} %collective-permute-done.12), channel_id=1, source_target_pairs={{0,1},{1,2},{2,3},{3,4},{4,5},{5,6},{6,7},{7,8},{8,9},{9,10},{10,1... | collective-permute-start | bytes 393224 | tf_op jit(solution)/shard_map/ppermute | solution.py:17
  72.9 2.6 copy-start
  242.7 39.6 %copy-start.3 = (f32[256,256]{1,0:T(8,128)S(1)}, f32[256,256]{1,0:T(8,128)}, u32[]{:S(2)}) copy-start(f32[256,256]{1,0:T(8,128)} %get-tuple-element.20) | copy-start | bytes 786436
  283.3 2.2 copy-start.2
  284.3 1.6 copy-start.1
Sparse Core Ops, SparseCore 0:
  78.2 140.5 all-reduce.3
